TPU v7x, 512 devices: a whole 4x4x16 slice. The times are simulated.
512 devices in a mesh: wa: 32 (over x, y, core), ha: 16 (over z).
Axes of the slice: x: 4, y: 4, z: 16, core: 2. Of those that a mesh axis runs over, the one named last changes fastest.
Arguments:
- residual_in: bfloat16 [192, 16384], P('ha', 'wa'), may hold values from -43.25 to 43.25
- grad_out: bfloat16 [192, 16384], P('ha', 'wa'), may hold values from -6 to 6
- norm_gain: bfloat16 [16384], P('wa'), may hold values from 0.099609375 to 1.8984375
- w_gate: bfloat16 [16384, 26624], P('wa', 'ha'), may hold values from -0.0390625 to 0.0390625
- w_up: bfloat16 [16384, 26624], P('wa', 'ha'), may hold values from -0.0390625 to 0.0390625
- w_down: bfloat16 [26624, 16384], P('ha', 'wa'), may hold values from -0.030643146 to 0.030643146
Outputs:
- grad_in: bfloat16 [192, 16384], P('ha', 'wa')
All inputs are finite; a program needn't handle non-finite values.
Results may differ from a plain program's by a relative error of at most 0.0053.
Values may be sent and summed in bfloat16 or wider, within the bound.
No kernel may reach another device: no remote copies, remote signals or barrier semaphores. Data moves between devices by JAX's collectives and lax.ppermute only.
A program may use at most 64 MiB of HBM per device.

v0:
```python
import jax
import jax.numpy as jnp
from jax import lax
from jax.sharding import PartitionSpec as P

D = 16384


def gate_grads(gate, up, d_hidden):
    sig = jax.nn.sigmoid(gate)
    d_up = (d_hidden * gate * sig).astype(jnp.bfloat16)
    d_gate = (d_hidden * up * sig * (1.0 + gate * (1.0 - sig))).astype(jnp.bfloat16)
    return jnp.stack([d_gate, d_up])


def local(residual_in, grad_out, norm_gain, w_gate, w_up, w_down):
    stream = residual_in.astype(jnp.float32)
    squares = lax.psum(jnp.sum(stream * stream, axis=1), "wa")
    inv_rms = lax.rsqrt(squares / D + 1e-05)[:, None]
    gain_f = norm_gain.astype(jnp.float32)
    normed = (stream * inv_rms * gain_f).astype(jnp.bfloat16)
    stacked = jnp.stack([normed, grad_out])
    piece = lax.all_gather(stacked, "ha", axis=1, tiled=True)
    gate_part = jnp.dot(piece[0], w_gate, preferred_element_type=jnp.float32)
    up_part = jnp.dot(piece[0], w_up, preferred_element_type=jnp.float32)
    back_part = lax.dot_general(
        piece[1], w_down, (((1,), (1,)), ((), ())), preferred_element_type=jnp.float32
    )
    partial_sums = jnp.stack([gate_part, up_part, back_part])
    summed = lax.psum(partial_sums, "wa")
    grads = gate_grads(summed[0], summed[1], summed[2])
    total = lax.dot_general(
        grads[0], w_gate, (((1,), (1,)), ((), ())), preferred_element_type=jnp.float32
    )
    d_normed = lax.psum_scatter(
        total
        + lax.dot_general(
            grads[1], w_up, (((1,), (1,)), ((), ())), preferred_element_type=jnp.float32
        ),
        "ha",
        scatter_dimension=0,
        tiled=True,
    )
    scaled = d_normed * gain_f
    row_dot = lax.psum(jnp.sum(scaled * stream, axis=1), "wa")[:, None]
    grad_in = grad_out.astype(jnp.float32) + inv_rms * scaled - stream * inv_rms**3 * row_dot / D
    return grad_in.astype(jnp.bfloat16)


def solution(mesh):
    placed = (P("ha", "wa"), P("ha", "wa"), P("wa"), P("wa", "ha"), P("wa", "ha"), P("ha", "wa"))
    return jax.shard_map(
        local, mesh=mesh, in_specs=placed, out_specs=P("ha", "wa"), check_vma=False
    )
```

profile of v0, /device:TPU:1, one launch (start us, length us, event | category | flops | bytes accessed | tf_op | source)
XLA Modules:
  0.0 384.8 jit_solution(6059536915146214695)
XLA Ops:
  6.5 1.0 fusion.8
  7.5 69.0 %psum.21 = f32[12]{0:T(128)S(1)} all-reduce(f32[12]{0:T(128)S(1)} %fusion.8), channel_id=1, replica_groups=mesh['wa'=32,'ha'=16] {'wa'}, use_global_device_ids=true, to_apply=%region_1.0 | all-reduce | flops 12 | bytes 96 | tf_op jit(solution)/shard_map/psum | solution.py:18
  76.5 0.7 convert_element_type.23
  77.2 0.8 fusion.16
  78.0 0.7 pad_maximum_fusion.1
  78.8 25.4 %all_gather.3 = bf16[2,192,512]{2,0,1:T(2,128)(2,1)S(1)} all-gather(bf16[2,12,512]{2,0,1:T(2,128)(2,1)S(1)} %copy.7), channel_id=1, replica_groups=mesh['wa'=32,'ha'=16] {'ha'}, dimensions={1}, use_global_device_ids=true | all-gather | bytes 417792 | tf_op jit(solution)/shard_map/all_gather | solution.py:23
  104.2 0.5 fusion.19
  104.7 0.5 convolution_bitcast_fusion.1
  105.3 0.5 convolution_bitcast_fusion.2
  105.8 0.9 copy-done.1
  106.7 0.7 convolution_bitcast_fusion
  107.4 2.1 pad_maximum_fusion
  109.6 143.8 %all-reduce.4.cloned.1.call-done = f32[3,192,1664]{2,1,0:T(8,128)} async-done(((f32[3,192,1664]{2,1,0:T(8,128)}), f32[3,192,1664]{2,1,0:T(8,128)}) %all-reduce.4.cloned.1.call-update) | async-done | bytes 3833872 | tf_op jit(solution)/shard_map/psum | solution.py:30
  253.4 2.8 fusion.6
  256.2 3.2 convolution_add_fusion
  259.5 29.2 %fusion = f32[16,512]{1,0:T(8,128)S(1)} fusion(f32[192,512]{1,0:T(8,128)} %convolution_add_fusion), kind=kCustom, calls=%all-reduce-scatter | all-reduce-scatter fusion | flops 131073 | bytes 428032
  288.7 1.7 collective-permute-start
  290.4 2.7 collective-permute-start.1
  293.2 4.9 %collective-permute-start.2 = (f32[16,512]{1,0:T(8,128)S(1)}, f32[16,512]{1,0:T(8,128)S(1)}, u32[]{:S(2)}, u32[]{:S(2)}) collective-permute-start(f32[16,512]{1,0:T(8,128)S(1)} %fusion), channel_id=1, source_target_pairs={{0,3},{1,4},{2,5},{3,6},{4,7},{5,8},{6,9},{7,10},{8,11},{9,12},{10... | collective-permute-start | bytes 98312
  298.1 5.6 %collective-permute-start.3 = (f32[12,512]{1,0:T(8,128)S(1)}, f32[12,512]{1,0:T(8,128)S(1)}, u32[]{:S(2)}, u32[]{:S(2)}) collective-permute-start(f32[12,512]{1,0:T(8,128)S(1)} %slice.26), channel_id=1, source_target_pairs={{0,4},{1,5},{2,6},{3,7},{4,8},{5,9},{6,10},{7,11},{8,12},{9,13},{1... | collective-permute-start | bytes 73736
  303.7 1.3 dynamic-slice.4
  305.6 0.5 concatenate
  306.3 71.0 %psum.23 = f32[12]{0:T(128)S(1)} all-reduce(f32[12]{0:T(128)S(1)} %fusion.15), channel_id=1, replica_groups=mesh['wa'=32,'ha'=16] {'wa'}, use_global_device_ids=true, to_apply=%region_5.0 | all-reduce | flops 12 | bytes 96 | tf_op jit(solution)/shard_map/psum | solution.py:45
  377.3 0.7 fusion.14
  (19 shorter events, 0.2 us)
Async XLA Ops:
  6.5 98.7 %copy-start = (bf16[512,1664]{1,0:T(8,128)(2,1)S(1)}, bf16[512,1664]{1,0:T(8,128)(2,1)}, u32[]{:S(2)}) copy-start(bf16[512,1664]{1,0:T(8,128)(2,1)} %param.9) | copy-start | bytes 5111812
  6.5 98.2 %copy-start.2 = (bf16[512,1664]{1,0:T(8,128)(2,1)S(1)}, bf16[512,1664]{1,0:T(8,128)(2,1)}, u32[]{:S(2)}) copy-start(bf16[512,1664]{1,0:T(8,128)(2,1)} %param.10) | copy-start | bytes 5111812
  6.5 246.9 %all-reduce.4.cloned.1.call-start = ((), (), s32[]{:S(2)}) async-start(), calls=%async_computation | async-start | bytes 7667712 | tf_op jit(solution)/shard_map/psum | solution.py:30
  105.3 1.5 copy-start.1
  256.2 50.0 %copy-start.3 = (bf16[12,512]{1,0:T(8,128)(2,1)S(1)}, bf16[12,512]{1,0:T(8,128)(2,1)}, u32[]{:S(2)}) copy-start(bf16[12,512]{1,0:T(8,128)(2,1)} %param.6) | copy-start | bytes 36868
  256.2 121.0 %copy-start.4 = (bf16[12,512]{1,0:T(8,128)(2,1)S(1)}, bf16[12,512]{1,0:T(8,128)(2,1)}, u32[]{:S(2)}) copy-start(bf16[12,512]{1,0:T(8,128)(2,1)} %param.7) | copy-start | bytes 36868
  288.7 16.9 %collective-permute-start = (f32[16,512]{1,0:T(8,128)S(1)}, f32[16,512]{1,0:T(8,128)S(1)}, u32[]{:S(2)}, u32[]{:S(2)}) collective-permute-start(f32[16,512]{1,0:T(8,128)S(1)} %fusion), channel_id=1, source_target_pairs={{0,1},{1,2},{2,3},{3,4},{4,5},{5,6},{6,7},{7,8},{8,9},{9,10},{10,1... | collective-permute-start | bytes 98312
  290.4 15.2 %collective-permute-start.1 = (f32[16,512]{1,0:T(8,128)S(1)}, f32[16,512]{1,0:T(8,128)S(1)}, u32[]{:S(2)}, u32[]{:S(2)}) collective-permute-start(f32[16,512]{1,0:T(8,128)S(1)} %fusion), channel_id=1, source_target_pairs={{0,2},{1,3},{2,4},{3,5},{4,6},{5,7},{6,8},{7,9},{8,10},{9,11},{10,... | collective-permute-start | bytes 98312
  293.2 12.5 %collective-permute-start.2 = (f32[16,512]{1,0:T(8,128)S(1)}, f32[16,512]{1,0:T(8,128)S(1)}, u32[]{:S(2)}, u32[]{:S(2)}) collective-permute-start(f32[16,512]{1,0:T(8,128)S(1)} %fusion), channel_id=1, source_target_pairs={{0,3},{1,4},{2,5},{3,6},{4,7},{5,8},{6,9},{7,10},{8,11},{9,12},{10... | collective-permute-start | bytes 98312
  298.1 7.5 %collective-permute-start.3 = (f32[12,512]{1,0:T(8,128)S(1)}, f32[12,512]{1,0:T(8,128)S(1)}, u32[]{:S(2)}, u32[]{:S(2)}) collective-permute-start(f32[12,512]{1,0:T(8,128)S(1)} %slice.26), channel_id=1, source_target_pairs={{0,4},{1,5},{2,6},{3,7},{4,8},{5,9},{6,10},{7,11},{8,12},{9,13},{1... | collective-permute-start | bytes 73736
Sparse Core Ops, SparseCore 0:
  109.7 143.6 all-reduce.3
where the time goes:
time: 385 us
  blocking collectives  195 us (51%)
  waiting for transfers between devices  144 us (37%)
  starting transfers between devices  14.9 us (4%)
  between operations  14.2 us (4%)
  matrix products  7.8 us (2%)
  other arithmetic  6.15 us (2%)
    psum x1, waiting for transfers between devices, local(): summed = lax.psum(partial_sums, 'wa')  144 us
    psum x1, blocking collectives, local(): row_dot = lax.psum(jnp.sum(scaled * stream, axis=1), 'wa')[:, None]  71 us
    psum x1, blocking collectives, local(): squares = lax.psum(jnp.sum(stream * stream, axis=1), 'wa')  69 us
    unnamed x1, blocking collectives  29.2 us
    all_gather x1, blocking collectives, local(): piece = lax.all_gather(stacked, 'ha', axis=1, tiled=True)  25.4 us
    unnamed x4, starting transfers between devices  14.9 us
  transfers between devices with their start and end apart: 5, of which 1 were waited for; matrix products, arithmetic and copies ran while one was open for 0% of the time, Pallas kernels for 0%

commit v1 on v0

--- a/solution.py
+++ b/solution.py
@@ -4,6 +4,15 @@
 from jax.sharding import PartitionSpec as P
 
 D = 16384
+
+
+def added_up(array, axis):
+    peers = lax.axis_size(axis)
+    total, stride = (array, 1)
+    while stride < peers:
+        total = total + lax.ppermute(total, axis, [(i, i ^ stride) for i in range(peers)])
+        stride = 2 * stride
+    return total
 
 
 def gate_grads(gate, up, d_hidden):
@@ -27,7 +36,7 @@
         piece[1], w_down, (((1,), (1,)), ((), ())), preferred_element_type=jnp.float32
     )
     partial_sums = jnp.stack([gate_part, up_part, back_part])
-    summed = lax.psum(partial_sums, "wa")
+    summed = added_up(partial_sums, "wa")
     grads = gate_grads(summed[0], summed[1], summed[2])
     total = lax.dot_general(
         grads[0], w_gate, (((1,), (1,)), ((), ())), preferred_element_type=jnp.float32

time: 385 us -> 585 us (1.52)
  waiting for transfers between devices: 144 us -> 340 us
  starting transfers between devices: 14.9 us -> 35.7 us
  between operations: 14.2 us -> 0.89 us
    ppermute x0 -> x5, waiting for transfers between devices: none -> 340 us  [added_up(): lax.ppermute(total, axis, [(i, i ^ stride) for i in range(peers)])]
    psum x1 -> x0, waiting for transfers between devices: 144 us -> none  [local(): summed = lax.psum(partial_sums, 'wa')]
    ppermute x0 -> x5, starting transfers between devices: none -> 21.7 us  [added_up(): lax.ppermute(total, axis, [(i, i ^ stride) for i in range(peers)])]
  transfers between devices with their start and end apart: 5 -> 9, of which waited for: 1 -> 5; matrix products, arithmetic and copies ran while one was open for 0% -> 0% of each run, Pallas kernels for 0% -> 0%
where the time goes in v1:
time: 585 us; the launch traced here: 584 us
  waiting for transfers between devices  340 us (58%)
  blocking collectives  194 us (33%)
  starting transfers between devices  35.7 us (6%)
  other arithmetic  6.3 us (1%)
    ppermute x5, waiting for transfers between devices, added_up(): lax.ppermute(total, axis, [(i, i ^ stride) for i in range(peers)])  340 us
    psum x1, blocking collectives, local(): row_dot = lax.psum(jnp.sum(scaled * stream, axis=1), 'wa')[:, None]  74.3 us
    psum x1, blocking collectives, local(): squares = lax.psum(jnp.sum(stream * stream, axis=1), 'wa')  68.9 us
    all_gather x1, blocking collectives, local(): piece = lax.all_gather(stacked, 'ha', axis=1, tiled=True)  25.4 us
    unnamed x1, blocking collectives  25.1 us
    ppermute x5, starting transfers between devices, added_up(): lax.ppermute(total, axis, [(i, i ^ stride) for i in range(peers)])  21.7 us
    unnamed x4, starting transfers between devices  14 us
  transfers between devices with their start and end apart: 9, of which 5 were waited for; matrix products, arithmetic and copies ran while one was open for 0% of the time, Pallas kernels for 0%

profile of v1, /device:TPU:1, one launch (start us, length us, event | category | flops | bytes accessed | tf_op | source)
XLA Modules:
  0.0 584.2 jit_solution(12726245433025709723)
XLA Ops:
  0.0 1.0 fusion.7
  1.0 68.9 %psum.14 = f32[12]{0:T(128)S(1)} all-reduce(f32[12]{0:T(128)S(1)} %fusion.7), channel_id=1, replica_groups=mesh['wa'=32,'ha'=16] {'wa'}, use_global_device_ids=true, to_apply=%region_1.0 | all-reduce | flops 12 | bytes 96 | tf_op jit(solution)/shard_map/psum | solution.py:27
  70.5 0.8 fusion.15
  72.1 25.4 %all_gather.3 = bf16[2,192,512]{2,0,1:T(2,128)(2,1)S(1)} all-gather(bf16[2,12,512]{2,0,1:T(2,128)(2,1)S(1)} %copy.7), channel_id=1, replica_groups=mesh['wa'=32,'ha'=16] {'ha'}, dimensions={1}, use_global_device_ids=true | all-gather | bytes 417792 | tf_op jit(solution)/shard_map/all_gather | solution.py:32
  98.6 0.9 copy-done.2
  100.0 0.9 copy-done.1
  101.9 14.0 %collective-permute-start = (f32[3,192,1664]{2,1,0:T(8,128)S(1)}, f32[3,192,1664]{2,1,0:T(8,128)S(1)}, u32[]{:S(2)}, u32[]{:S(2)}) collective-permute-start(f32[3,192,1664]{2,1,0:T(8,128)S(1)} %pad_maximum_fusion), channel_id=1, source_target_pairs={{0,16},{16,0},{32,48},{48,32},{64,80},{80,64},{96,112},{112,96},{1... | collective-permute-start | bytes 11501576 | tf_op jit(solution)/shard_map/ppermute | solution.py:13
  115.9 6.2 %collective-permute-done = f32[3,192,1664]{2,1,0:T(8,128)S(1)} collective-permute-done((f32[3,192,1664]{2,1,0:T(8,128)S(1)}, f32[3,192,1664]{2,1,0:T(8,128)S(1)}, u32[]{:S(2)}, u32[]{:S(2)}) %collective-permute-start) | collective-permute-done | bytes 3833888 | tf_op jit(solution)/shard_map/ppermute | solution.py:13
  122.6 1.9 collective-permute-start.1
  124.5 84.0 %collective-permute-done.1 = f32[3,192,1664]{2,1,0:T(8,128)S(1)} collective-permute-done((f32[3,192,1664]{2,1,0:T(8,128)S(1)}, f32[3,192,1664]{2,1,0:T(8,128)S(1)}, u32[]{:S(2)}, u32[]{:S(2)}) %collective-permute-start.1) | collective-permute-done | bytes 3833888 | tf_op jit(solution)/shard_map/ppermute | solution.py:13
  209.0 1.9 collective-permute-start.2
  211.0 84.6 %collective-permute-done.2 = f32[3,192,1664]{2,1,0:T(8,128)S(1)} collective-permute-done((f32[3,192,1664]{2,1,0:T(8,128)S(1)}, f32[3,192,1664]{2,1,0:T(8,128)S(1)}, u32[]{:S(2)}, u32[]{:S(2)}) %collective-permute-start.2) | collective-permute-done | bytes 3833888 | tf_op jit(solution)/shard_map/ppermute | solution.py:13
  296.0 1.9 collective-permute-start.3
  297.9 82.3 %collective-permute-done.3 = f32[3,192,1664]{2,1,0:T(8,128)S(1)} collective-permute-done((f32[3,192,1664]{2,1,0:T(8,128)S(1)}, f32[3,192,1664]{2,1,0:T(8,128)S(1)}, u32[]{:S(2)}, u32[]{:S(2)}) %collective-permute-start.3) | collective-permute-done | bytes 3833888 | tf_op jit(solution)/shard_map/ppermute | solution.py:13
  380.6 1.9 collective-permute-start.4
  382.5 82.9 %collective-permute-done.4 = f32[3,192,1664]{2,1,0:T(8,128)S(1)} collective-permute-done((f32[3,192,1664]{2,1,0:T(8,128)S(1)}, f32[3,192,1664]{2,1,0:T(8,128)S(1)}, u32[]{:S(2)}, u32[]{:S(2)}) %collective-permute-start.4) | collective-permute-done | bytes 3833888 | tf_op jit(solution)/shard_map/ppermute | solution.py:13
  466.6 0.8 convolution_add_fusion
  467.5 25.1 %fusion = f32[16,512]{1,0:T(8,128)S(1)} fusion(f32[192,512]{1,0:T(8,128)S(1)} %convolution_add_fusion), kind=kCustom, calls=%all-reduce-scatter | all-reduce-scatter fusion | flops 131073 | bytes 428032
  492.6 2.1 collective-permute-start.5
  494.6 1.7 collective-permute-start.6
  496.4 4.3 collective-permute-start.7
  500.7 5.9 %collective-permute-start.8 = (f32[12,512]{1,0:T(8,128)S(1)}, f32[12,512]{1,0:T(8,128)S(1)}, u32[]{:S(2)}, u32[]{:S(2)}) collective-permute-start(f32[12,512]{1,0:T(8,128)S(1)} %slice.26), channel_id=1, source_target_pairs={{0,4},{1,5},{2,6},{3,7},{4,8},{5,9},{6,10},{7,11},{8,12},{9,13},{1... | collective-permute-start | bytes 73736
  506.6 1.3 dynamic-slice.4
  509.2 74.3 %psum.15 = f32[12]{0:T(128)S(1)} all-reduce(f32[12]{0:T(128)S(1)} %fusion.14), channel_id=1, replica_groups=mesh['wa'=32,'ha'=16] {'wa'}, use_global_device_ids=true, to_apply=%region_4.0 | all-reduce | flops 12 | bytes 96 | tf_op jit(solution)/shard_map/psum | solution.py:54
  (31 shorter events, 8.2 us)
Async XLA Ops:
  0.0 98.0 %copy-start = (bf16[512,1664]{1,0:T(8,128)(2,1)S(1)}, bf16[512,1664]{1,0:T(8,128)(2,1)}, u32[]{:S(2)}) copy-start(bf16[512,1664]{1,0:T(8,128)(2,1)} %param.10) | copy-start | bytes 5111812
  98.0 1.5 copy-start.2
  99.5 1.5 copy-start.1
  101.9 20.3 %collective-permute-start = (f32[3,192,1664]{2,1,0:T(8,128)S(1)}, f32[3,192,1664]{2,1,0:T(8,128)S(1)}, u32[]{:S(2)}, u32[]{:S(2)}) collective-permute-start(f32[3,192,1664]{2,1,0:T(8,128)S(1)} %pad_maximum_fusion), channel_id=1, source_target_pairs={{0,16},{16,0},{32,48},{48,32},{64,80},{80,64},{96,112},{112,96},{1... | collective-permute-start | bytes 11501576 | tf_op jit(solution)/shard_map/ppermute | solution.py:13
  122.6 85.9 %collective-permute-start.1 = (f32[3,192,1664]{2,1,0:T(8,128)S(1)}, f32[3,192,1664]{2,1,0:T(8,128)S(1)}, u32[]{:S(2)}, u32[]{:S(2)}) collective-permute-start(f32[3,192,1664]{2,1,0:T(8,128)S(1)} %fusion.18), channel_id=1, source_target_pairs={{0,32},{16,48},{32,0},{48,16},{64,96},{80,112},{96,64},{112,80},{1... | collective-permute-start | bytes 11501576 | tf_op jit(solution)/shard_map/ppermute | solution.py:13
  209.0 86.6 %collective-permute-start.2 = (f32[3,192,1664]{2,1,0:T(8,128)S(1)}, f32[3,192,1664]{2,1,0:T(8,128)S(1)}, u32[]{:S(2)}, u32[]{:S(2)}) collective-permute-start(f32[3,192,1664]{2,1,0:T(8,128)S(1)} %fusion.25), channel_id=1, source_target_pairs={{0,64},{16,80},{32,96},{48,112},{64,0},{80,16},{96,32},{112,48},{1... | collective-permute-start | bytes 11501576 | tf_op jit(solution)/shard_map/ppermute | solution.py:13
  296.0 84.2 %collective-permute-start.3 = (f32[3,192,1664]{2,1,0:T(8,128)S(1)}, f32[3,192,1664]{2,1,0:T(8,128)S(1)}, u32[]{:S(2)}, u32[]{:S(2)}) collective-permute-start(f32[3,192,1664]{2,1,0:T(8,128)S(1)} %add.39), channel_id=1, source_target_pairs={{0,128},{16,144},{32,160},{48,176},{64,192},{80,208},{96,224},{112... | collective-permute-start | bytes 11501576 | tf_op jit(solution)/shard_map/ppermute | solution.py:13
  380.6 84.9 %collective-permute-start.4 = (f32[3,192,1664]{2,1,0:T(8,128)S(1)}, f32[3,192,1664]{2,1,0:T(8,128)S(1)}, u32[]{:S(2)}, u32[]{:S(2)}) collective-permute-start(f32[3,192,1664]{2,1,0:T(8,128)S(1)} %add.40), channel_id=1, source_target_pairs={{0,256},{16,272},{32,288},{48,304},{64,320},{80,336},{96,352},{112... | collective-permute-start | bytes 11501576 | tf_op jit(solution)/shard_map/ppermute | solution.py:13
  466.6 42.5 %copy-start.3 = (bf16[12,512]{1,0:T(8,128)(2,1)S(1)}, bf16[12,512]{1,0:T(8,128)(2,1)}, u32[]{:S(2)}) copy-start(bf16[12,512]{1,0:T(8,128)(2,1)} %param.6) | copy-start | bytes 36868
  466.6 116.9 %copy-start.4 = (bf16[12,512]{1,0:T(8,128)(2,1)S(1)}, bf16[12,512]{1,0:T(8,128)(2,1)}, u32[]{:S(2)}) copy-start(bf16[12,512]{1,0:T(8,128)(2,1)} %param.7) | copy-start | bytes 36868
  492.6 16.0 %collective-permute-start.5 = (f32[16,512]{1,0:T(8,128)S(1)}, f32[16,512]{1,0:T(8,128)S(1)}, u32[]{:S(2)}, u32[]{:S(2)}) collective-permute-start(f32[16,512]{1,0:T(8,128)S(1)} %fusion), channel_id=1, source_target_pairs={{0,1},{1,2},{2,3},{3,4},{4,5},{5,6},{6,7},{7,8},{8,9},{9,10},{10,1... | collective-permute-start | bytes 98312
  494.6 13.9 %collective-permute-start.6 = (f32[16,512]{1,0:T(8,128)S(1)}, f32[16,512]{1,0:T(8,128)S(1)}, u32[]{:S(2)}, u32[]{:S(2)}) collective-permute-start(f32[16,512]{1,0:T(8,128)S(1)} %fusion), channel_id=1, source_target_pairs={{0,2},{1,3},{2,4},{3,5},{4,6},{5,7},{6,8},{7,9},{8,10},{9,11},{10,... | collective-permute-start | bytes 98312
  496.4 12.2 %collective-permute-start.7 = (f32[16,512]{1,0:T(8,128)S(1)}, f32[16,512]{1,0:T(8,128)S(1)}, u32[]{:S(2)}, u32[]{:S(2)}) collective-permute-start(f32[16,512]{1,0:T(8,128)S(1)} %fusion), channel_id=1, source_target_pairs={{0,3},{1,4},{2,5},{3,6},{4,7},{5,8},{6,9},{7,10},{8,11},{9,12},{10... | collective-permute-start | bytes 98312
  500.7 7.8 %collective-permute-start.8 = (f32[12,512]{1,0:T(8,128)S(1)}, f32[12,512]{1,0:T(8,128)S(1)}, u32[]{:S(2)}, u32[]{:S(2)}) collective-permute-start(f32[12,512]{1,0:T(8,128)S(1)} %slice.26), channel_id=1, source_target_pairs={{0,4},{1,5},{2,6},{3,7},{4,8},{5,9},{6,10},{7,11},{8,12},{9,13},{1... | collective-permute-start | bytes 73736
